TPU v7x, 512 devices: a whole 4x8x8 slice. The times are simulated.
512 devices in a mesh: dp: 16 (over y, core), comp: 32 (over z, x).
Axes of the slice: x: 4, y: 8, z: 8, core: 2. Of those that a mesh axis runs over, the one named last changes fastest.
Arguments:
- descriptors: bfloat16 [65536, 256], P('dp'), may hold values from -12 to 12
- means: float32 [16384, 256], P('comp'), may hold values from -3 to 3
- variances: float32 [16384, 256], P('comp'), may hold values from 0.5 to 2
- log_weights: float32 [16384], P('comp'), may hold values from -2 to 2
Outputs:
- new_log_weights: float32 [16384], P('comp')
- new_means: float32 [16384, 256], P('comp')
- new_variances: float32 [16384, 256], P('comp')
All inputs are finite; a program needn't handle non-finite values.
Results may differ from a plain program's by a relative error of at most 0.002.
Values sent between devices are 32-bit elements; how exact they have to be, the bound alone decides.
No kernel may reach another device: no remote copies, remote signals or barrier semaphores. Data moves between devices by JAX's collectives and lax.ppermute only.
A program may use at most 64 MiB of HBM per device.

v0:
```python
import jax
import jax.numpy as jnp
from jax import lax
from jax.sharding import PartitionSpec as P

prior_count = 1.0
log_two_pi = 1.8378770664093453


def finish(moments, counts, means, variances, grand_total):
    feature_width = means.shape[1]
    weight = counts + prior_count
    new_means = (moments[:, :feature_width] + prior_count * means) / weight[:, None]
    new_variances = (
        moments[:, feature_width:] + prior_count * (variances + means * means)
    ) / weight[:, None] - new_means * new_means
    new_log_weights = jnp.log(weight) - jnp.log(grand_total)
    return (new_log_weights, new_means, new_variances)


def on_device(descriptors, means, variances, log_weights):
    row_count = descriptors.shape[0]
    feature_width = descriptors.shape[1]
    owned_count = means.shape[0]
    grand_total = row_count * lax.axis_size("dp") + prior_count * owned_count * lax.axis_size(
        "comp"
    )
    precision = 1.0 / variances
    scaled_means = means * precision
    loading = jnp.concatenate([-0.5 * precision, scaled_means], axis=1)
    offset = log_weights - 0.5 * jnp.sum(
        means * scaled_means + jnp.log(variances) + log_two_pi, axis=1
    )
    block_rows = min(512, row_count)
    stacked = descriptors.reshape(row_count // block_rows, block_rows, feature_width)

    def score_block(row_block):
        exact = row_block.astype(jnp.float32)
        features = jnp.concatenate([exact * exact, exact], axis=1)
        return (
            lax.dot_general(
                features,
                loading,
                (((1,), (1,)), ((), ())),
                precision=lax.Precision.HIGHEST,
                preferred_element_type=jnp.float32,
            )
            + offset[None, :]
        )

    scores = lax.map(score_block, stacked).reshape(row_count, owned_count)
    local_max = jnp.max(scores, axis=1)
    local_sum = jnp.sum(jnp.exp(scores - local_max[:, None]), axis=1)
    gathered = lax.all_gather(jnp.stack([local_max, local_sum]), "comp")
    row_max = jnp.max(gathered[:, 0], axis=0)
    row_sum = jnp.sum(gathered[:, 1] * jnp.exp(gathered[:, 0] - row_max[None, :]), axis=0)
    log_total = row_max + jnp.log(row_sum)
    responsibility = jnp.exp(scores - log_total[:, None])
    counts = jnp.sum(responsibility, axis=0)
    resp_half = responsibility.astype(jnp.bfloat16)
    exact_rows = descriptors.astype(jnp.float32)
    halves = jnp.concatenate([descriptors, (exact_rows * exact_rows).astype(jnp.bfloat16)], axis=1)
    moments = lax.dot_general(
        resp_half, halves, (((0,), (0,)), ((), ())), preferred_element_type=jnp.float32
    )
    packed = lax.psum(jnp.concatenate([moments, counts[None, :]], axis=0), "dp")
    summed_moments = packed[:owned_count]
    summed_counts = packed[owned_count]
    new_log_weights, new_means, new_variances = finish(
        summed_moments, summed_counts, means, variances, grand_total
    )
    return (new_log_weights, new_means, new_variances)


def solution(mesh):
    placed = (P("dp", None), P("comp", None), P("comp", None), P("comp"))
    return jax.shard_map(
        on_device,
        mesh=mesh,
        in_specs=placed,
        out_specs=(P("comp"), P("comp", None), P("comp", None)),
        check_vma=False,
    )
```

profile of v0, /device:TPU:25, one launch (start us, length us, event | category | flops | bytes accessed | tf_op | source)
XLA Modules:
  0.0 273.0 jit_solution(8249931385995249936)
XLA Ops:
  7.2 0.0 copy-start.5
  7.2 0.0 copy-start
  7.2 0.0 all-gather.4.cloned.1.call-start
  7.2 1.6 add_reduce_fusion
  8.8 0.1 pad_maximum_fusion.1
  9.0 0.0 copy-done.5
  9.0 0.1 copy-done
  9.1 23.7 %while.10 = (s32[]{:T(128)}, f32[8,512,512]{2,1,0:T(8,128)}, bf16[8,512,256]{2,1,0:T(8,128)(2,1)S(1)}, f32[512,512]{1,0:T(8,128)S(1)}, f32[512]{0:T(512)S(1)}, /*index=5*/s32[]{:T(128)}) while((s32[]{:T(128)}, f32[8,512,512]{2,1,0:T(8,128)}, bf16[8,512,256]{2,1,0:T(8,128)(2,1)S(1)}, f32[512,512]{1,0:T(8,128)S(1)}, f32[512]{0:T(512)S(1)}, ...), condition=%wide.region_2.3_spmd, body=%wide.region_1.2_spmd.sunk | while | flops 1611530240 | bytes 4721229 | solution.py:51
  9.2 2.9 %fusion.32 = f32[8,512,512]{2,1,0:T(8,128)} fusion(f32[8,512,512]{2,1,0:T(8,128)} %get-tuple-element.87, s32[]{:T(128)} %get-tuple-element.86, f32[512,512]{1,0:T(8,128)S(1)} %get-tuple-element.95, f32[512,256]{1,0:T(8,128)S(1)} %bitcast_convert_fusion.2, f32[512,256]{1,0:T(8,128)S(1)} %fusion.31, f32[512]{0:T(512)S(1)} %get-tuple-element.96), kind=kOutput, calls=%fused_computation.2.clone.1 | convolution fusion | flops 1611137024 | bytes 3148288 | tf_op jit(solution)/shard_map/while/body/eval_jaxpr/dot_general | solution.py:41
  12.1 2.9 %fusion.32 = f32[8,512,512]{2,1,0:T(8,128)} fusion(f32[8,512,512]{2,1,0:T(8,128)} %get-tuple-element.87, s32[]{:T(128)} %get-tuple-element.86, f32[512,512]{1,0:T(8,128)S(1)} %get-tuple-element.95, f32[512,256]{1,0:T(8,128)S(1)} %bitcast_convert_fusion.2, f32[512,256]{1,0:T(8,128)S(1)} %fusion.31, f32[512]{0:T(512)S(1)} %get-tuple-element.96), kind=kOutput, calls=%fused_computation.2.clone.1 | convolution fusion | flops 1611137024 | bytes 3148288 | tf_op jit(solution)/shard_map/while/body/eval_jaxpr/dot_general | solution.py:41
  15.1 2.9 %fusion.32 = f32[8,512,512]{2,1,0:T(8,128)} fusion(f32[8,512,512]{2,1,0:T(8,128)} %get-tuple-element.87, s32[]{:T(128)} %get-tuple-element.86, f32[512,512]{1,0:T(8,128)S(1)} %get-tuple-element.95, f32[512,256]{1,0:T(8,128)S(1)} %bitcast_convert_fusion.2, f32[512,256]{1,0:T(8,128)S(1)} %fusion.31, f32[512]{0:T(512)S(1)} %get-tuple-element.96), kind=kOutput, calls=%fused_computation.2.clone.1 | convolution fusion | flops 1611137024 | bytes 3148288 | tf_op jit(solution)/shard_map/while/body/eval_jaxpr/dot_general | solution.py:41
  18.1 2.9 %fusion.32 = f32[8,512,512]{2,1,0:T(8,128)} fusion(f32[8,512,512]{2,1,0:T(8,128)} %get-tuple-element.87, s32[]{:T(128)} %get-tuple-element.86, f32[512,512]{1,0:T(8,128)S(1)} %get-tuple-element.95, f32[512,256]{1,0:T(8,128)S(1)} %bitcast_convert_fusion.2, f32[512,256]{1,0:T(8,128)S(1)} %fusion.31, f32[512]{0:T(512)S(1)} %get-tuple-element.96), kind=kOutput, calls=%fused_computation.2.clone.1 | convolution fusion | flops 1611137024 | bytes 3148288 | tf_op jit(solution)/shard_map/while/body/eval_jaxpr/dot_general | solution.py:41
  21.0 2.8 %fusion.32 = f32[8,512,512]{2,1,0:T(8,128)} fusion(f32[8,512,512]{2,1,0:T(8,128)} %get-tuple-element.87, s32[]{:T(128)} %get-tuple-element.86, f32[512,512]{1,0:T(8,128)S(1)} %get-tuple-element.95, f32[512,256]{1,0:T(8,128)S(1)} %bitcast_convert_fusion.2, f32[512,256]{1,0:T(8,128)S(1)} %fusion.31, f32[512]{0:T(512)S(1)} %get-tuple-element.96), kind=kOutput, calls=%fused_computation.2.clone.1 | convolution fusion | flops 1611137024 | bytes 3148288 | tf_op jit(solution)/shard_map/while/body/eval_jaxpr/dot_general | solution.py:41
  24.0 2.9 %fusion.32 = f32[8,512,512]{2,1,0:T(8,128)} fusion(f32[8,512,512]{2,1,0:T(8,128)} %get-tuple-element.87, s32[]{:T(128)} %get-tuple-element.86, f32[512,512]{1,0:T(8,128)S(1)} %get-tuple-element.95, f32[512,256]{1,0:T(8,128)S(1)} %bitcast_convert_fusion.2, f32[512,256]{1,0:T(8,128)S(1)} %fusion.31, f32[512]{0:T(512)S(1)} %get-tuple-element.96), kind=kOutput, calls=%fused_computation.2.clone.1 | convolution fusion | flops 1611137024 | bytes 3148288 | tf_op jit(solution)/shard_map/while/body/eval_jaxpr/dot_general | solution.py:41
  27.0 2.9 %fusion.32 = f32[8,512,512]{2,1,0:T(8,128)} fusion(f32[8,512,512]{2,1,0:T(8,128)} %get-tuple-element.87, s32[]{:T(128)} %get-tuple-element.86, f32[512,512]{1,0:T(8,128)S(1)} %get-tuple-element.95, f32[512,256]{1,0:T(8,128)S(1)} %bitcast_convert_fusion.2, f32[512,256]{1,0:T(8,128)S(1)} %fusion.31, f32[512]{0:T(512)S(1)} %get-tuple-element.96), kind=kOutput, calls=%fused_computation.2.clone.1 | convolution fusion | flops 1611137024 | bytes 3148288 | tf_op jit(solution)/shard_map/while/body/eval_jaxpr/dot_general | solution.py:41
  29.9 2.8 %fusion.32 = f32[8,512,512]{2,1,0:T(8,128)} fusion(f32[8,512,512]{2,1,0:T(8,128)} %get-tuple-element.87, s32[]{:T(128)} %get-tuple-element.86, f32[512,512]{1,0:T(8,128)S(1)} %get-tuple-element.95, f32[512,256]{1,0:T(8,128)S(1)} %bitcast_convert_fusion.2, f32[512,256]{1,0:T(8,128)S(1)} %fusion.31, f32[512]{0:T(512)S(1)} %get-tuple-element.96), kind=kOutput, calls=%fused_computation.2.clone.1 | convolution fusion | flops 1611137024 | bytes 3148288 | tf_op jit(solution)/shard_map/while/body/eval_jaxpr/dot_general | solution.py:41
  32.8 4.0 %reduce_max.18 = f32[8,512]{1,0:T(8,128)S(1)} reduce(f32[8,512,512]{2,1,0:T(8,128)} %get-tuple-element.30, f32[]{:T(128)} %constant.10.clone.1), dimensions={2}, to_apply=%region_3.4 | reduce | flops 2093056 | bytes 8404996 | tf_op jit(solution)/shard_map/reduce_max | solution.py:52
  36.8 4.4 %exponential_reduce_fusion.1 = f32[8,512]{1,0:T(8,128)S(1)} fusion(f32[8,512,512]{2,1,0:T(8,128)} %get-tuple-element.30, f32[8,512]{1,0:T(8,128)S(1)} %reduce_max.18), kind=kLoop, calls=%fused_computation.13 | loop fusion | flops 4190208 | bytes 8421376 | tf_op jit(solution)/shard_map/reduce_sum | solution.py:53
  41.3 0.6 maximum_bitcast_fusion
  41.9 0.0 all-gather.4.cloned.1.call-update
  41.9 0.0 all-reduce.2.cloned.1.call-start
  42.0 1.8 multiply_convert_fusion
  43.8 79.9 %all-gather.4.cloned.1.call-done = f32[32,2,4096]{2,1,0:T(2,128)} async-done(((f32[1,2,4096]{2,1,0:T(2,128)}), f32[32,2,4096]{2,1,0:T(2,128)}) %all-gather.4.cloned.1.call-update) | async-done | bytes 1048592 | tf_op jit(solution)/shard_map/all_gather | solution.py:54
  123.7 2.9 %fusion.22 = (f32[32,1,4096]{2,1,0:T(1,128)S(1)}, f32[4096]{0:T(1024)S(1)}, f32[32,1,4096]{2,1,0:T(1,128)S(1)}) fusion(f32[32,2,4096]{2,1,0:T(2,128)} %all-gather.4.cloned.1.call-done), kind=kLoop, calls=%fused_computation.42 | loop fusion | flops 126976 | bytes 2113536 | tf_op jit(solution)/shard_map/slice | solution.py:55
  126.6 0.7 fusion.17
  127.4 5.4 %fusion.8 = bf16[4096,512]{1,0:T(8,128)(2,1)} fusion(f32[8,512,512]{2,1,0:T(8,128)} %get-tuple-element.30, f32[4096]{0:T(1024)S(1)} %log_add_fusion), kind=kLoop, calls=%fused_computation.11 | loop fusion | flops 4194304 | bytes 12599296 | tf_op jit(solution)/shard_map/convert_element_type | solution.py:60
  132.8 0.0 copy-start.1
  132.8 0.0 copy-start.2
  132.8 4.2 %exponential_reduce_fusion = f32[512]{0:T(512)S(1)} fusion(f32[8,512,512]{2,1,0:T(8,128)} %get-tuple-element.30, f32[8,512]{1,0:T(8,128)S(1)} %add.60), kind=kLoop, calls=%fused_computation.12 | loop fusion | flops 4193792 | bytes 8407040 | tf_op jit(solution)/shard_map/reduce_sum | solution.py:59
  137.0 0.4 copy-done.1
  137.4 0.7 copy-done.2
  138.1 0.0 copy-start.3
  138.1 0.0 copy-start.4
  138.1 2.3 fusion.9
  140.4 1.1 pad_maximum_fusion
  141.5 0.0 all-reduce.2.cloned.1.call-update
  141.6 121.0 %all-reduce.2.cloned.1.call-done = f32[513,512]{1,0:T(8,128)} async-done(((f32[513,512]{1,0:T(8,128)}), f32[513,512]{1,0:T(8,128)}) %all-reduce.2.cloned.1.call-update) | async-done | bytes 1050640 | tf_op jit(solution)/shard_map/psum | solution.py:66
  262.5 0.7 slice_add_fusion.2
  263.3 0.6 log_add_fusion.1
  263.8 0.0 copy-done.3
  263.8 0.0 copy-done.4
  263.8 2.4 fusion.14
  (22 shorter events, 0.7 us)
Async XLA Ops:
  7.2 1.8 copy-start.5
  7.2 1.9 copy-start
  7.2 116.5 %all-gather.4.cloned.1.call-start = ((), (), s32[]{:S(2)}) async-start(), calls=%async_computation.1 | async-start | bytes 1081344 | tf_op jit(solution)/shard_map/all_gather | solution.py:54
  41.9 220.6 %all-reduce.2.cloned.1.call-start = ((), (), s32[]{:S(2)}) async-start(), calls=%async_computation | async-start | bytes 2129920 | tf_op jit(solution)/shard_map/psum | solution.py:66
  132.8 4.6 %copy-start.1 = (bf16[4096,512]{1,0:T(8,128)(2,1)S(1)}, bf16[4096,512]{1,0:T(8,128)(2,1)}, u32[]{:S(2)}) copy-start(bf16[4096,512]{1,0:T(8,128)(2,1)} %fusion.8) | copy-start | bytes 12582916
  132.8 5.3 %copy-start.2 = (bf16[4096,256]{1,0:T(8,128)(2,1)S(1)}, bf16[4096,256]{1,0:T(8,128)(2,1)}, u32[]{:S(2)}) copy-start(bf16[4096,256]{1,0:T(8,128)(2,1)} %multiply_convert_fusion) | copy-start | bytes 6291460
  138.1 125.8 %copy-start.3 = (f32[512,256]{1,0:T(8,128)S(1)}, f32[512,256]{1,0:T(8,128)}, u32[]{:S(2)}) copy-start(f32[512,256]{1,0:T(8,128)} %param.8) | copy-start | bytes 1572868
  138.1 125.8 %copy-start.4 = (f32[512,256]{1,0:T(8,128)S(1)}, f32[512,256]{1,0:T(8,128)}, u32[]{:S(2)}) copy-start(f32[512,256]{1,0:T(8,128)} %param.7) | copy-start | bytes 1572868
Sparse Core Ops, SparseCore 0:
  42.1 81.5 all-gather.3
  141.7 120.7 all-reduce.1
where the time goes:
time: 273 us
  waiting for transfers between devices  201 us (74%)
  other arithmetic  31.3 us (11%)
  matrix products  25.3 us (9%)
  between operations  14.2 us (5%)
    psum x1, waiting for transfers between devices, on_device(): packed = lax.psum(jnp.concatenate([moments, counts[None, :]], axis=0), 'dp')  121 us
    all_gather x1, waiting for transfers between devices, on_device(): gathered = lax.all_gather(jnp.stack([local_max, local_sum]), 'comp')  79.9 us
    dot_general x8, matrix products, score_block(): lax.dot_general(features, loading, (((1,), (1,)), ((), ())), precision=la...  22.9 us
  transfers between devices with their start and end apart: 2, of which 2 were waited for; matrix products, arithmetic and copies ran while one was open for 1% of the time, Pallas kernels for 0%

commit v1 on v0

--- a/solution.py
+++ b/solution.py
@@ -63,7 +63,9 @@
     moments = lax.dot_general(
         resp_half, halves, (((0,), (0,)), ((), ())), preferred_element_type=jnp.float32
     )
-    packed = lax.psum(jnp.concatenate([moments, counts[None, :]], axis=0), "dp")
+    packed = jnp.sum(
+        lax.all_gather(jnp.concatenate([moments, counts[None, :]], axis=0), "dp"), axis=0
+    )
     summed_moments = packed[:owned_count]
     summed_counts = packed[owned_count]
     new_log_weights, new_means, new_variances = finish(

time: 273 us -> 261 us (0.956)
  the two profiles are of different devices: /device:TPU:25 before, /device:TPU:1 now
where the time goes in v1:
time: 261 us
  waiting for transfers between devices  183 us (70%)
  other arithmetic  37.5 us (14%)
  matrix products  25.3 us (10%)
  between operations  14.2 us (5%)
    all_gather x1, waiting for transfers between devices, on_device(): lax.all_gather(jnp.concatenate([moments, counts[None, :]], axis=0), 'dp')  102 us
    all_gather x1, waiting for transfers between devices, on_device(): gathered = lax.all_gather(jnp.stack([local_max, local_sum]), 'comp')  80.8 us
    dot_general x8, matrix products, score_block(): lax.dot_general(features, loading, (((1,), (1,)), ((), ())), precision=la...  22.9 us
    reduce_sum x1, other arithmetic, on_device(): jnp.sum(lax.all_gather(jnp.concatenate([moments, counts[None, :]], axis=0...  8.09 us
    convert_element_type x1, other arithmetic, on_device(): resp_half = responsibility.astype(jnp.bfloat16)  5.39 us
  transfers between devices with their start and end apart: 2, of which 2 were waited for; matrix products, arithmetic and copies ran while one was open for 1% of the time, Pallas kernels for 0%

profile of v1, /device:TPU:1, one launch (start us, length us, event | category | flops | bytes accessed | tf_op | source)
XLA Modules:
  0.0 261.2 jit_solution(9567194248315664066)
XLA Ops:
  7.2 0.0 copy-start.5
  7.2 0.0 copy-start
  7.2 0.0 all-gather.7.cloned.1.call-start
  7.2 1.6 add_reduce_fusion
  8.8 0.1 pad_maximum_fusion
  9.0 0.0 copy-done.5
  9.0 0.1 copy-done
  9.1 23.7 %while.10 = (s32[]{:T(128)}, f32[8,512,512]{2,1,0:T(8,128)}, bf16[8,512,256]{2,1,0:T(8,128)(2,1)S(1)}, f32[512,512]{1,0:T(8,128)S(1)}, f32[512]{0:T(512)S(1)}, /*index=5*/s32[]{:T(128)}) while((s32[]{:T(128)}, f32[8,512,512]{2,1,0:T(8,128)}, bf16[8,512,256]{2,1,0:T(8,128)(2,1)S(1)}, f32[512,512]{1,0:T(8,128)S(1)}, f32[512]{0:T(512)S(1)}, ...), condition=%wide.region_2.3_spmd, body=%wide.region_1.2_spmd.sunk | while | flops 1611530240 | bytes 4721229 | solution.py:51
  9.2 2.9 %fusion.32 = f32[8,512,512]{2,1,0:T(8,128)} fusion(f32[8,512,512]{2,1,0:T(8,128)} %get-tuple-element.87, s32[]{:T(128)} %get-tuple-element.86, f32[512,512]{1,0:T(8,128)S(1)} %get-tuple-element.95, f32[512,256]{1,0:T(8,128)S(1)} %bitcast_convert_fusion.2, f32[512,256]{1,0:T(8,128)S(1)} %fusion.31, f32[512]{0:T(512)S(1)} %get-tuple-element.96), kind=kOutput, calls=%fused_computation.2.clone.1 | convolution fusion | flops 1611137024 | bytes 3148288 | tf_op jit(solution)/shard_map/while/body/eval_jaxpr/dot_general | solution.py:41
  12.1 2.9 %fusion.32 = f32[8,512,512]{2,1,0:T(8,128)} fusion(f32[8,512,512]{2,1,0:T(8,128)} %get-tuple-element.87, s32[]{:T(128)} %get-tuple-element.86, f32[512,512]{1,0:T(8,128)S(1)} %get-tuple-element.95, f32[512,256]{1,0:T(8,128)S(1)} %bitcast_convert_fusion.2, f32[512,256]{1,0:T(8,128)S(1)} %fusion.31, f32[512]{0:T(512)S(1)} %get-tuple-element.96), kind=kOutput, calls=%fused_computation.2.clone.1 | convolution fusion | flops 1611137024 | bytes 3148288 | tf_op jit(solution)/shard_map/while/body/eval_jaxpr/dot_general | solution.py:41
  15.1 2.9 %fusion.32 = f32[8,512,512]{2,1,0:T(8,128)} fusion(f32[8,512,512]{2,1,0:T(8,128)} %get-tuple-element.87, s32[]{:T(128)} %get-tuple-element.86, f32[512,512]{1,0:T(8,128)S(1)} %get-tuple-element.95, f32[512,256]{1,0:T(8,128)S(1)} %bitcast_convert_fusion.2, f32[512,256]{1,0:T(8,128)S(1)} %fusion.31, f32[512]{0:T(512)S(1)} %get-tuple-element.96), kind=kOutput, calls=%fused_computation.2.clone.1 | convolution fusion | flops 1611137024 | bytes 3148288 | tf_op jit(solution)/shard_map/while/body/eval_jaxpr/dot_general | solution.py:41
  18.1 2.9 %fusion.32 = f32[8,512,512]{2,1,0:T(8,128)} fusion(f32[8,512,512]{2,1,0:T(8,128)} %get-tuple-element.87, s32[]{:T(128)} %get-tuple-element.86, f32[512,512]{1,0:T(8,128)S(1)} %get-tuple-element.95, f32[512,256]{1,0:T(8,128)S(1)} %bitcast_convert_fusion.2, f32[512,256]{1,0:T(8,128)S(1)} %fusion.31, f32[512]{0:T(512)S(1)} %get-tuple-element.96), kind=kOutput, calls=%fused_computation.2.clone.1 | convolution fusion | flops 1611137024 | bytes 3148288 | tf_op jit(solution)/shard_map/while/body/eval_jaxpr/dot_general | solution.py:41
  21.0 2.8 %fusion.32 = f32[8,512,512]{2,1,0:T(8,128)} fusion(f32[8,512,512]{2,1,0:T(8,128)} %get-tuple-element.87, s32[]{:T(128)} %get-tuple-element.86, f32[512,512]{1,0:T(8,128)S(1)} %get-tuple-element.95, f32[512,256]{1,0:T(8,128)S(1)} %bitcast_convert_fusion.2, f32[512,256]{1,0:T(8,128)S(1)} %fusion.31, f32[512]{0:T(512)S(1)} %get-tuple-element.96), kind=kOutput, calls=%fused_computation.2.clone.1 | convolution fusion | flops 1611137024 | bytes 3148288 | tf_op jit(solution)/shard_map/while/body/eval_jaxpr/dot_general | solution.py:41
  24.0 2.9 %fusion.32 = f32[8,512,512]{2,1,0:T(8,128)} fusion(f32[8,512,512]{2,1,0:T(8,128)} %get-tuple-element.87, s32[]{:T(128)} %get-tuple-element.86, f32[512,512]{1,0:T(8,128)S(1)} %get-tuple-element.95, f32[512,256]{1,0:T(8,128)S(1)} %bitcast_convert_fusion.2, f32[512,256]{1,0:T(8,128)S(1)} %fusion.31, f32[512]{0:T(512)S(1)} %get-tuple-element.96), kind=kOutput, calls=%fused_computation.2.clone.1 | convolution fusion | flops 1611137024 | bytes 3148288 | tf_op jit(solution)/shard_map/while/body/eval_jaxpr/dot_general | solution.py:41
  27.0 2.9 %fusion.32 = f32[8,512,512]{2,1,0:T(8,128)} fusion(f32[8,512,512]{2,1,0:T(8,128)} %get-tuple-element.87, s32[]{:T(128)} %get-tuple-element.86, f32[512,512]{1,0:T(8,128)S(1)} %get-tuple-element.95, f32[512,256]{1,0:T(8,128)S(1)} %bitcast_convert_fusion.2, f32[512,256]{1,0:T(8,128)S(1)} %fusion.31, f32[512]{0:T(512)S(1)} %get-tuple-element.96), kind=kOutput, calls=%fused_computation.2.clone.1 | convolution fusion | flops 1611137024 | bytes 3148288 | tf_op jit(solution)/shard_map/while/body/eval_jaxpr/dot_general | solution.py:41
  29.9 2.8 %fusion.32 = f32[8,512,512]{2,1,0:T(8,128)} fusion(f32[8,512,512]{2,1,0:T(8,128)} %get-tuple-element.87, s32[]{:T(128)} %get-tuple-element.86, f32[512,512]{1,0:T(8,128)S(1)} %get-tuple-element.95, f32[512,256]{1,0:T(8,128)S(1)} %bitcast_convert_fusion.2, f32[512,256]{1,0:T(8,128)S(1)} %fusion.31, f32[512]{0:T(512)S(1)} %get-tuple-element.96), kind=kOutput, calls=%fused_computation.2.clone.1 | convolution fusion | flops 1611137024 | bytes 3148288 | tf_op jit(solution)/shard_map/while/body/eval_jaxpr/dot_general | solution.py:41
  32.8 4.0 %reduce_max.18 = f32[8,512]{1,0:T(8,128)S(1)} reduce(f32[8,512,512]{2,1,0:T(8,128)} %get-tuple-element.30, f32[]{:T(128)} %constant.10.clone.1), dimensions={2}, to_apply=%region_3.4 | reduce | flops 2093056 | bytes 8404996 | tf_op jit(solution)/shard_map/reduce_max | solution.py:52
  36.8 4.4 %exponential_reduce_fusion.1 = f32[8,512]{1,0:T(8,128)S(1)} fusion(f32[8,512,512]{2,1,0:T(8,128)} %get-tuple-element.30, f32[8,512]{1,0:T(8,128)S(1)} %reduce_max.18), kind=kLoop, calls=%fused_computation.13 | loop fusion | flops 4190208 | bytes 8421376 | tf_op jit(solution)/shard_map/reduce_sum | solution.py:53
  41.3 0.6 maximum_bitcast_fusion.1
  41.9 0.0 all-gather.7.cloned.1.call-update
  41.9 0.2 all-gather.9.cloned.1.call-start
  42.2 1.8 multiply_convert_fusion
  43.9 80.8 %all-gather.7.cloned.1.call-done = f32[32,2,4096]{2,1,0:T(2,128)} async-done(((f32[1,2,4096]{2,1,0:T(2,128)}), f32[32,2,4096]{2,1,0:T(2,128)}) %all-gather.7.cloned.1.call-update) | async-done | bytes 1048592 | tf_op jit(solution)/shard_map/all_gather | solution.py:54
  124.8 2.9 %fusion.22 = (f32[32,1,4096]{2,1,0:T(1,128)S(1)}, f32[4096]{0:T(1024)S(1)}, f32[32,1,4096]{2,1,0:T(1,128)S(1)}) fusion(f32[32,2,4096]{2,1,0:T(2,128)} %all-gather.7.cloned.1.call-done), kind=kLoop, calls=%fused_computation.42 | loop fusion | flops 126976 | bytes 2113536 | tf_op jit(solution)/shard_map/slice | solution.py:55
  127.7 0.7 fusion.17
  128.4 5.4 %fusion.8 = bf16[4096,512]{1,0:T(8,128)(2,1)} fusion(f32[8,512,512]{2,1,0:T(8,128)} %get-tuple-element.30, f32[4096]{0:T(1024)S(1)} %log_add_fusion), kind=kLoop, calls=%fused_computation.11 | loop fusion | flops 4194304 | bytes 12599296 | tf_op jit(solution)/shard_map/convert_element_type | solution.py:60
  133.8 0.0 copy-start.1
  133.8 0.0 copy-start.2
  133.9 4.2 %exponential_reduce_fusion = f32[512]{0:T(512)S(1)} fusion(f32[8,512,512]{2,1,0:T(8,128)} %get-tuple-element.30, f32[8,512]{1,0:T(8,128)S(1)} %add.58), kind=kLoop, calls=%fused_computation.12 | loop fusion | flops 4193792 | bytes 8407040 | tf_op jit(solution)/shard_map/reduce_sum | solution.py:59
  138.1 0.4 copy-done.1
  138.5 0.7 copy-done.2
  139.2 2.3 fusion.9
  141.5 1.1 maximum_bitcast_fusion
  142.6 0.0 all-gather.9.cloned.1.call-update
  142.6 0.0 copy-start.3
  142.6 0.0 copy-start.4
  142.6 101.8 %all-gather.9.cloned.1.call-done = f32[16,513,512]{2,1,0:T(8,128)} async-done(((f32[1,513,512]{2,1,0:T(8,128)}), f32[16,513,512]{2,1,0:T(8,128)}) %all-gather.9.cloned.1.call-update) | async-done | bytes 16810000 | tf_op jit(solution)/shard_map/all_gather | solution.py:67
  244.5 8.1 %reduce_sum.49 = f32[513,512]{1,0:T(8,128)S(1)} reduce(f32[16,513,512]{2,1,0:T(8,128)} %all-gather.9.cloned.1.call-done, f32[]{:T(128)} %constant.4.clone.1), dimensions={0}, to_apply=%region_8.9 | reduce | flops 3939840 | bytes 17860612 | tf_op jit(solution)/shard_map/reduce_sum | solution.py:66
  252.6 0.0 copy-done.3
  252.6 0.0 copy-done.4
  252.6 1.2 fusion.14
  253.7 0.6 log_add_fusion.1
  (23 shorter events, 0.7 us)
Async XLA Ops:
  7.2 1.8 copy-start.5
  7.2 1.9 copy-start
  7.2 117.6 %all-gather.7.cloned.1.call-start = ((), (), s32[]{:S(2)}) async-start(), calls=%async_computation | async-start | bytes 1081344 | tf_op jit(solution)/shard_map/all_gather | solution.py:54
  41.9 202.5 %all-gather.9.cloned.1.call-start = ((), (), s32[]{:S(2)}) async-start(), calls=%async_computation.1 | async-start | bytes 18104320 | tf_op jit(solution)/shard_map/all_gather | solution.py:67
  133.8 4.6 %copy-start.1 = (bf16[4096,512]{1,0:T(8,128)(2,1)S(1)}, bf16[4096,512]{1,0:T(8,128)(2,1)}, u32[]{:S(2)}) copy-start(bf16[4096,512]{1,0:T(8,128)(2,1)} %fusion.8) | copy-start | bytes 12582916
  133.8 5.3 %copy-start.2 = (bf16[4096,256]{1,0:T(8,128)(2,1)S(1)}, bf16[4096,256]{1,0:T(8,128)(2,1)}, u32[]{:S(2)}) copy-start(bf16[4096,256]{1,0:T(8,128)(2,1)} %multiply_convert_fusion) | copy-start | bytes 6291460
  142.6 110.0 %copy-start.3 = (f32[512,256]{1,0:T(8,128)S(1)}, f32[512,256]{1,0:T(8,128)}, u32[]{:S(2)}) copy-start(f32[512,256]{1,0:T(8,128)} %param.8) | copy-start | bytes 1572868
  142.6 110.0 %copy-start.4 = (f32[512,256]{1,0:T(8,128)S(1)}, f32[512,256]{1,0:T(8,128)}, u32[]{:S(2)}) copy-start(f32[512,256]{1,0:T(8,128)} %param.7) | copy-start | bytes 1572868
Sparse Core Ops, SparseCore 0:
  42.1 82.6 all-gather.6
  142.7 101.6 all-gather.8
